TPU v7x, 32 devices: a whole 2x2x4 slice. The times are simulated.
32 devices in a mesh: freq: 4 (over y, core), row: 8 (over z, x).
Axes of the slice: x: 2, y: 2, z: 4, core: 2. Of those that a mesh axis runs over, the one named last changes fastest.
Arguments:
- traces: bfloat16 [2, 8192, 8192], P(None, ('freq', 'row')), may hold values from -1.1953125 to 1.1953125
- prior: bfloat16 [4, 2, 8192, 8192], P('freq', None, None, 'row'), may hold values from -0.796875 to 0.796875
- bins: int32 [4], replicated, may hold values from 64 to 255
- panels: int32 [2], replicated, may hold values from 0 to 31
Outputs:
- multiples: bfloat16 [4, 2, 8192, 8192], P('freq', None, 'row')
- spectrum: bfloat16 [4, 2, 8192, 8192], P('freq', None, None, 'row')
All inputs are finite; a program needn't handle non-finite values.
Results may differ from a plain program's by a relative error of at most 0.0077.
Values may be sent and summed in bfloat16 or wider, within the bound.
No kernel may reach another device: no remote copies, remote signals or barrier semaphores. Data moves between devices by JAX's collectives and lax.ppermute only.
A program may use at most 640 MiB of HBM per device.

v0:
```python
import math
import jax
import jax.numpy as jnp
from jax import lax
from jax.sharding import PartitionSpec as P

NT_REC = 1024
PANEL = 256
STEPS = 2
BLOCK_START = 1022


def spread(value, axis, source):
    kept = jnp.where(lax.axis_index(axis) == source, value, 0).astype(value.dtype)
    return lax.psum(kept, axis)


def complex_terms(left, right):
    dims = (((0,), (1,)), ((), ()))

    def product(first, second):
        return lax.dot_general(first, second, dims, preferred_element_type=jnp.float32)

    real_part = product(left[0], right[0]) - product(left[1], right[1])
    imag_part = product(left[0], right[1]) + product(left[1], right[0])
    return (real_part, imag_part)


def body(traces, prior, bins, panels):
    sample_count, shots_local, receivers = traces.shape
    row_count = lax.axis_size("row")
    block_rows = receivers // row_count
    sample_index = BLOCK_START + jnp.arange(sample_count, dtype=jnp.int32)
    turn_count = bins[:, None] * sample_index[None, :] % NT_REC
    angles = 2.0 * math.pi / NT_REC * turn_count.astype(jnp.float32)
    twiddle = jnp.stack([jnp.cos(angles), -jnp.sin(angles)], axis=1).astype(jnp.bfloat16)
    own_twiddle = lax.dynamic_index_in_dim(twiddle, lax.axis_index("freq"), 0, keepdims=False)
    by_row = lax.all_to_all(traces, "row", split_axis=2, concat_axis=1, tiled=True)
    gathered = lax.all_gather(by_row, "freq", axis=1, tiled=True)
    transformed = jnp.einsum(
        "tsb,ct->csb", gathered, own_twiddle, preferred_element_type=jnp.float32
    ).astype(jnp.bfloat16)
    spectrum = (prior[0].astype(jnp.float32) + transformed.astype(jnp.float32)).astype(jnp.bfloat16)
    panels_each = block_rows // PANEL
    real_sum = jnp.zeros((block_rows, receivers), jnp.float32)
    imag_sum = jnp.zeros((block_rows, receivers), jnp.float32)
    for panel_step in range(STEPS):
        chosen = panels[panel_step]
        owner = chosen // panels_each
        offset = chosen % panels_each * PANEL
        own_rows = lax.dynamic_slice_in_dim(spectrum, offset, PANEL, 2)
        panel_data = spread(own_rows, "row", owner)
        left = lax.dynamic_slice_in_dim(spectrum, chosen * PANEL, PANEL, 1)
        real_part, imag_part = complex_terms(left, panel_data)
        real_sum = real_sum + real_part
        imag_sum = imag_sum + imag_part
    return (jnp.stack([real_sum, imag_sum])[None].astype(jnp.bfloat16), spectrum[None])


def solution(mesh):
    return jax.shard_map(
        body,
        mesh=mesh,
        in_specs=(P(None, ("freq", "row"), None), P("freq", None, None, "row"), P(), P()),
        out_specs=(P("freq", None, "row", None), P("freq", None, None, "row")),
        check_vma=False,
    )
```

profile of v0, /device:TPU:0, one launch (start us, length us, event | category | flops | bytes accessed | tf_op | source)
XLA Modules:
  0.0 1370.1 jit_solution(301745803882222178)
XLA Ops:
  7.2 0.0 all-gather.2.cloned.1.call-start
  7.2 21.0 %copy.21 = bf16[2,256,8192]{1,0,2:T(2,128)(2,1)} copy(bf16[2,256,8192]{2,1,0:T(8,128)(2,1)} %param.4) | data formatting | bytes 16777216 | tf_op args[0]
  28.2 190.4 %all_to_all.18 = bf16[2,256,8192]{1,0,2:T(2,128)(2,1)} all-to-all(bf16[2,256,8192]{1,0,2:T(2,128)(2,1)} %copy.21), channel_id=1, replica_groups=mesh['freq'=4,'row'=8] {'row'}, dimensions={2} | all-to-all | bytes 16777216 | tf_op jit(solution)/shard_map/all_to_all | solution.py:38
  218.6 30.5 %copy.22 = bf16[2,8,256,1024]{3,0,2,1:T(2,128)(2,1)} copy(bf16[2,8,256,1024]{2,0,3,1:T(2,128)(2,1)} %bitcast.60) | data formatting | bytes 16777216 | tf_op jit(solution)/shard_map/all_to_all | solution.py:38
  249.1 0.0 copy-start.1
  249.1 0.0 copy-start.2
  249.1 0.0 all-gather.2.cloned.1.call-update
  249.1 0.0 all-reduce.3.cloned.1.call-start
  249.2 0.6 copy-done.1
  249.8 0.6 fusion.49
  255.3 0.0 copy-done.2
  255.3 0.1 cosine_convert_fusion
  255.4 0.2 fusion.45
  255.6 194.4 %all-gather.2.cloned.1.call-done = bf16[2,8192,1024]{2,0,1:T(2,128)(2,1)} async-done(((bf16[2,2048,1024]{2,0,1:T(2,128)(2,1)}), bf16[2,8192,1024]{2,0,1:T(2,128)(2,1)}) %all-gather.2.cloned.1.call-update) | async-done | bytes 33554448 | tf_op jit(solution)/shard_map/all_gather | solution.py:39
  449.9 145.3 %fusion = bf16[2,8192,1024]{2,0,1:T(2,128)(2,1)} fusion(bf16[1,2,8192,1024]{3,2,1,0:T(8,128)(2,1)} %param.5, bf16[2,8192,1024]{2,0,1:T(2,128)(2,1)} %all-gather.2.cloned.1.call-done, bf16[2,2]{1,0:T(2,128)(2,1)S(1)} %fusion.45), kind=kOutput, calls=%fused_computation.1 | convolution fusion | flops 150994944 | bytes 100663304 | tf_op jit(solution)/shard_map/tsb,ct->csb/dot_general | solution.py:40
  595.3 17.1 %broadcast_select_fusion.1 = (bf16[2,8192,256]{2,0,1:T(2,128)(2,1)}, bf16[2,8192,256]{2,0,1:T(2,128)(2,1)}) fusion(pred[]{:T(512)S(6)} %eq.11, bf16[2,8192,1024]{2,0,1:T(2,128)(2,1)} %fusion, s32[]{:T(128)S(6)} %select_n.71, s32[]{:T(128)S(6)} %select_n.77, pred[]{:T(512)S(6)} %eq.12), kind=kLoop, calls=%fused_computation.7 | loop fusion | flops 8388608 | bytes 33554440 | tf_op jit(solution)/shard_map/jit(_where)/select_n | solution.py:14
  612.3 0.0 all-reduce.3.cloned.1.call-update
  613.6 23.4 %copy.23 = bf16[1,2,8192,1024]{3,2,1,0:T(8,128)(2,1)} copy(bf16[1,2,8192,1024]{3,1,2,0:T(2,128)(2,1)} %bitcast.58) | data formatting | bytes 67108864
  637.0 6.3 constant_dynamic-slice_fusion.3
  643.3 479.6 %all-reduce.3.cloned.1.call-done = (bf16[2,8192,256]{2,0,1:T(2,128)(2,1)}, bf16[2,8192,256]{2,0,1:T(2,128)(2,1)}) async-done(((bf16[2,8192,256]{2,0,1:T(2,128)(2,1)}, bf16[2,8192,256]{2,0,1:T(2,128)(2,1)}), (bf16[2,8192,256]{2,0,1:T(2,128)(2,1)}, bf16[2,8192,256]{2,0,1:T(2,128)(2,1)})) %all-reduce.3.cloned.1.call-update) | async-done | bytes 16777232 | tf_op jit(solution)/shard_map/psum | solution.py:15
  1122.9 33.0 %fusion.47 = (bf16[1,8192,256]{2,0,1:T(2,128)(2,1)}, bf16[1,8192,256]{2,0,1:T(2,128)(2,1)}, bf16[1,8192,256]{2,0,1:T(2,128)(2,1)}, bf16[1,8192,256]{2,0,1:T(2,128)(2,1)}) fusion(bf16[2,8192,256]{2,0,1:T(2,128)(2,1)} %get-tuple-element.12, bf16[2,8192,256]{2,0,1:T(2,128)(2,1)} %get-tuple-element.13), kind=kLoop, calls=%fused_computation.67 | loop fusion | bytes 33554432 | tf_op jit(solution)/shard_map/slice | solution.py:24
  1155.9 0.0 copy-start
  1155.9 19.5 %fusion.11 = f32[1024,8192]{1,0:T(8,128)} fusion(bf16[1,8192,256]{2,0,1:T(2,128)(2,1)} %get-tuple-element.28, bf16[1,256,1024]{2,0,1:T(2,128)(2,1)} %get-tuple-element.17), kind=kOutput, calls=%fused_computation.18 | convolution fusion | flops 4294967296 | bytes 38273024 | tf_op jit(solution)/shard_map/dot_general | solution.py:22
  1175.3 0.0 copy-done
  1175.3 16.5 %fusion.13 = f32[1024,8192]{1,0:T(8,128)} fusion(bf16[1,8192,256]{2,0,1:T(2,128)(2,1)} %get-tuple-element.29, bf16[1,256,1024]{2,0,1:T(2,128)(2,1)S(1)} %copy-done), kind=kOutput, calls=%fused_computation.20 | convolution fusion | flops 4294967296 | bytes 38273024 | tf_op jit(solution)/shard_map/dot_general | solution.py:22
  1191.9 16.5 %fusion.15 = f32[1024,8192]{1,0:T(8,128)} fusion(bf16[1,8192,256]{2,0,1:T(2,128)(2,1)} %get-tuple-element.29, bf16[1,256,1024]{2,0,1:T(2,128)(2,1)S(1)} %get-tuple-element.16), kind=kOutput, calls=%fused_computation.22 | convolution fusion | flops 4294967296 | bytes 38273024 | tf_op jit(solution)/shard_map/dot_general | solution.py:22
  1208.4 16.5 %fusion.9 = f32[1024,8192]{1,0:T(8,128)} fusion(bf16[1,8192,256]{2,0,1:T(2,128)(2,1)} %get-tuple-element.28, bf16[1,256,1024]{2,0,1:T(2,128)(2,1)S(1)} %get-tuple-element.16), kind=kOutput, calls=%fused_computation.16 | convolution fusion | flops 4294967296 | bytes 38273024 | tf_op jit(solution)/shard_map/dot_general | solution.py:22
  1225.0 16.5 %fusion.7 = f32[1024,8192]{1,0:T(8,128)} fusion(bf16[1,8192,256]{2,0,1:T(2,128)(2,1)} %get-tuple-element.20, bf16[1,256,1024]{2,0,1:T(2,128)(2,1)S(1)} %get-tuple-element.15), kind=kOutput, calls=%fused_computation.14 | convolution fusion | flops 4294967296 | bytes 38273024 | tf_op jit(solution)/shard_map/dot_general | solution.py:22
  1241.5 17.5 %fusion.3 = f32[1024,8192]{1,0:T(8,128)} fusion(bf16[1,8192,256]{2,0,1:T(2,128)(2,1)} %get-tuple-element.21, bf16[1,256,1024]{2,0,1:T(2,128)(2,1)S(1)} %get-tuple-element.15), kind=kOutput, calls=%fused_computation.10 | convolution fusion | flops 4294967296 | bytes 38273024 | tf_op jit(solution)/shard_map/dot_general | solution.py:22
  1259.0 40.7 %fusion.1 = bf16[1,1,1024,8192]{3,2,1,0:T(8,128)(2,1)} fusion(f32[1024,8192]{1,0:T(8,128)} %fusion.7, f32[1024,8192]{1,0:T(8,128)} %fusion.15, f32[1024,8192]{1,0:T(8,128)} %fusion.11, bf16[1,8192,256]{2,0,1:T(2,128)(2,1)} %get-tuple-element.21, bf16[1,256,1024]{2,0,1:T(2,128)(2,1)S(1)} %get-tuple-element.14), kind=kOutput, calls=%fused_computation.8 | convolution fusion | flops 4328521728 | bytes 122159104 | tf_op jit(solution)/shard_map/dot_general | solution.py:22
  1299.7 40.6 %fusion.2 = bf16[1,1,1024,8192]{3,2,1,0:T(8,128)(2,1)} fusion(f32[1024,8192]{1,0:T(8,128)} %fusion.3, f32[1024,8192]{1,0:T(8,128)} %fusion.9, f32[1024,8192]{1,0:T(8,128)} %fusion.13, bf16[1,8192,256]{2,0,1:T(2,128)(2,1)} %get-tuple-element.20, bf16[1,256,1024]{2,0,1:T(2,128)(2,1)S(1)} %get-tuple-element.14), kind=kOutput, calls=%fused_computation.9 | convolution fusion | flops 4328521728 | bytes 122159104 | tf_op jit(solution)/shard_map/dot_general | solution.py:22
  1340.3 23.0 %pad_maximum_fusion = bf16[1,2,1024,8192]{3,2,1,0:T(8,128)(2,1)} fusion(bf16[1,1,1024,8192]{3,2,1,0:T(8,128)(2,1)} %fusion.2, bf16[1,1,1024,8192]{3,2,1,0:T(8,128)(2,1)} %fusion.1), kind=kLoop, calls=%fused_computation.3 | loop fusion | flops 16777216 | bytes 67108864 | tf_op jit(solution)/shard_map/stack | solution.py:57
  (1 shorter events, 0.0 us)
Async XLA Ops:
  7.2 442.8 %all-gather.2.cloned.1.call-start = ((), (), s32[]{:S(2)}) async-start(), calls=%async_computation.1 | async-start | bytes 41943040 | tf_op jit(solution)/shard_map/all_gather | solution.py:39
  249.1 0.7 copy-start.1
  249.1 6.2 copy-start.2
  249.1 873.8 %all-reduce.3.cloned.1.call-start = ((), (), s32[]{:S(2)}) async-start(), calls=%async_computation.2 | async-start | bytes 33554432 | tf_op jit(solution)/shard_map/psum | solution.py:15
  1155.9 19.5 %copy-start = (bf16[1,256,1024]{2,0,1:T(2,128)(2,1)S(1)}, bf16[1,256,1024]{2,0,1:T(2,128)(2,1)}, u32[]{:S(2)}) copy-start(bf16[1,256,1024]{2,0,1:T(2,128)(2,1)} %get-tuple-element.17) | copy-start | bytes 1572868
Sparse Core Ops, SparseCore 0:
  249.2 200.6 all-gather.1
  612.5 510.3 all-reduce.2
where the time goes:
time: 1370 us
  waiting for transfers between devices  674 us (49%)
  matrix products  330 us (24%)
  blocking collectives  190 us (14%)
  local copies, waits for them, and re-layouts  115 us (8%)
  other arithmetic  40.3 us (3%)
  between operations  20.2 us (1%)
    psum x1, waiting for transfers between devices, spread(): return lax.psum(kept, axis)  480 us
    all_gather x1, waiting for transfers between devices, body(): gathered = lax.all_gather(by_row, 'freq', axis=1, tiled=True)  194 us
    all_to_all x1, blocking collectives, body(): lax.all_to_all(traces, 'row', split_axis=2, concat_axis=1, tiled=True)  190 us
    dot_general x8, matrix products, product(): lax.dot_general(first, second, dims, preferred_element_type=jnp.float32)  184 us
    dot_general x1, matrix products, body(): jnp.einsum('tsb,ct->csb', gathered, own_twiddle, preferred_element_type=j...  145 us
    unnamed x8, local copies, waits for them, and re-layouts  45 us
    slice x2, local copies, waits for them, and re-layouts, complex_terms(): real_part = product(left[0], right[0]) - product(left[1], right[1])  39.3 us
    all_to_all x1, local copies, waits for them, and re-layouts, body(): lax.all_to_all(traces, 'row', split_axis=2, concat_axis=1, tiled=True)  30.5 us
  transfers between devices with their start and end apart: 2, of which 2 were waited for; matrix products, arithmetic and copies ran while one was open for 2% of the time, Pallas kernels for 0%

commit v1 on v0

--- a/solution.py
+++ b/solution.py
@@ -1,3 +1,4 @@
+import functools
 import math
 import jax
 import jax.numpy as jnp
@@ -8,6 +9,24 @@
 PANEL = 256
 STEPS = 2
 BLOCK_START = 1022
+
+
+def track_stacks_all(load, join_dim):
+    n_axis = jax.lax.axis_size("freq")
+    so_far_all = tuple(((d, (d + 1) % n_axis) for d in range(n_axis)))
+
+    def _view_domain(o_now):
+        if len(o_now) == n_axis:
+            return o_now
+        val2 = _view_domain([jax.lax.ppermute(o_now[0], "freq", so_far_all), *o_now])
+        return val2
+
+    after = jnp.concatenate(_view_domain([load]), axis=join_dim)
+    m_next = jnp.roll(after, (jax.lax.axis_index("freq") + 1) * load.shape[join_dim], axis=join_dim)
+    return m_next
+
+
+follow_orders_over_axis = functools.partial(track_stacks_all, join_dim=1)
 
 
 def spread(value, axis, source):
@@ -36,7 +55,7 @@
     twiddle = jnp.stack([jnp.cos(angles), -jnp.sin(angles)], axis=1).astype(jnp.bfloat16)
     own_twiddle = lax.dynamic_index_in_dim(twiddle, lax.axis_index("freq"), 0, keepdims=False)
     by_row = lax.all_to_all(traces, "row", split_axis=2, concat_axis=1, tiled=True)
-    gathered = lax.all_gather(by_row, "freq", axis=1, tiled=True)
+    gathered = follow_orders_over_axis(by_row)
     transformed = jnp.einsum(
         "tsb,ct->csb", gathered, own_twiddle, preferred_element_type=jnp.float32
     ).astype(jnp.bfloat16)

time: 1370 us -> 1520 us (1.11)
  waiting for transfers between devices: 674 us -> 752 us
  local copies, waits for them, and re-layouts: 115 us -> 178 us
    ppermute x0 -> x3, waiting for transfers between devices: none -> 273 us  [_view_domain(): jax.lax.ppermute(o_now[0], 'freq', so_far_all)]
    all_gather x1 -> x0, waiting for transfers between devices: 194 us -> none  [body(): gathered = lax.all_gather(by_row, 'freq', axis=1, tiled=True)]
    unnamed x8 -> x25, local copies, waits for them, and re-layouts: 45 us -> 101 us
  transfers between devices with their start and end apart: 2 -> 4, of which waited for: 2 -> 4; matrix products, arithmetic and copies ran while one was open for 2% -> 2% of each run, Pallas kernels for 0% -> 0%
where the time goes in v1:
time: 1520 us; the launch traced here: 1510 us
  waiting for transfers between devices  752 us (49%)
  matrix products  330 us (22%)
  blocking collectives  191 us (13%)
  local copies, waits for them, and re-layouts  178 us (12%)
  other arithmetic  40.3 us (3%)
  between operations  20.7 us (1%)
    psum x1, waiting for transfers between devices, spread(): return lax.psum(kept, axis)  479 us
    ppermute x3, waiting for transfers between devices, _view_domain(): jax.lax.ppermute(o_now[0], 'freq', so_far_all)  273 us
    all_to_all x1, blocking collectives, body(): lax.all_to_all(traces, 'row', split_axis=2, concat_axis=1, tiled=True)  191 us
    dot_general x8, matrix products, product(): lax.dot_general(first, second, dims, preferred_element_type=jnp.float32)  185 us
    dot_general x1, matrix products, body(): jnp.einsum('tsb,ct->csb', gathered, own_twiddle, preferred_element_type=j...  145 us
    unnamed x25, local copies, waits for them, and re-layouts  101 us
    slice x2, local copies, waits for them, and re-layouts, complex_terms(): real_part = product(left[0], right[0]) - product(left[1], right[1])  39.3 us
    all_to_all x1, local copies, waits for them, and re-layouts, body(): lax.all_to_all(traces, 'row', split_axis=2, concat_axis=1, tiled=True)  30.5 us
  transfers between devices with their start and end apart: 4, of which 4 were waited for; matrix products, arithmetic and copies ran while one was open for 2% of the time, Pallas kernels for 0%

profile of v1, /device:TPU:0, one launch (start us, length us, event | category | flops | bytes accessed | tf_op | source)
XLA Modules:
  0.0 1512.1 jit_solution(3943576727587876362)
XLA Ops:
  7.2 0.0 all-reduce.3.cloned.1.call-start
  7.2 21.0 %copy.21 = bf16[2,256,8192]{1,0,2:T(2,128)(2,1)} copy(bf16[2,256,8192]{2,1,0:T(8,128)(2,1)} %param.4) | data formatting | bytes 16777216 | tf_op args[0]
  28.2 0.0 copy-start.2
  28.2 0.0 copy-start.3
  28.2 190.6 %all_to_all.18 = bf16[2,256,8192]{1,0,2:T(2,128)(2,1)} all-to-all(bf16[2,256,8192]{1,0,2:T(2,128)(2,1)} %copy.21), channel_id=1, replica_groups=mesh['freq'=4,'row'=8] {'row'}, dimensions={2} | all-to-all | bytes 16777216 | tf_op jit(solution)/shard_map/all_to_all | solution.py:57
  218.8 30.5 %copy.22 = bf16[2,256,8,1024]{3,0,1,2:T(2,128)(2,1)} copy(bf16[2,256,8,1024]{1,0,3,2:T(2,128)(2,1)} %bitcast.67) | data formatting | bytes 16777216 | tf_op jit(solution)/shard_map/all_to_all | solution.py:57
  249.3 0.0 collective-permute-start
  249.3 93.1 %collective-permute-done = bf16[2,2048,1024]{2,0,1:T(2,128)(2,1)S(1)} collective-permute-done((bf16[2,2048,1024]{2,0,1:T(2,128)(2,1)}, bf16[2,2048,1024]{2,0,1:T(2,128)(2,1)S(1)}, u32[]{:S(2)}, u32[]{:S(2)}) %collective-permute-start) | collective-permute-done | bytes 8388640 | tf_op jit(solution)/shard_map/ppermute | solution.py:21
  342.3 0.0 copy-start
  342.3 3.4 copy-done
  345.7 0.0 collective-permute-start.1
  345.7 93.0 %collective-permute-done.1 = bf16[2,2048,1024]{2,0,1:T(2,128)(2,1)} collective-permute-done((bf16[2,2048,1024]{2,0,1:T(2,128)(2,1)S(1)}, bf16[2,2048,1024]{2,0,1:T(2,128)(2,1)}, u32[]{:S(2)}, u32[]{:S(2)}) %collective-permute-start.1) | collective-permute-done | bytes 8388640 | tf_op jit(solution)/shard_map/ppermute | solution.py:21
  438.7 0.0 collective-permute-start.2
  438.7 0.0 copy-done.2
  438.7 0.6 fusion.53
  444.4 0.0 copy-done.3
  444.4 0.1 cosine_convert_fusion
  444.5 0.0 slice-start.2
  444.5 0.2 fusion.49
  444.7 0.0 slice-start.3
  444.7 87.2 %collective-permute-done.2 = bf16[2,2048,1024]{2,0,1:T(2,128)(2,1)} collective-permute-done((bf16[2,2048,1024]{2,0,1:T(2,128)(2,1)}, bf16[2,2048,1024]{2,0,1:T(2,128)(2,1)}, u32[]{:S(2)}, u32[]{:S(2)}) %collective-permute-start.2) | collective-permute-done | bytes 8388640 | tf_op jit(solution)/shard_map/ppermute | solution.py:21
  531.9 8.0 constant_dynamic-update-slice_fusion.7
  539.9 0.0 slice-start
  539.9 8.1 constant_dynamic-update-slice_fusion.6
  548.1 0.0 slice-done.2
  548.1 0.0 slice-done.3
  548.1 0.0 slice-start.1
  548.1 7.0 constant_dynamic-update-slice_fusion.5
  555.1 0.0 slice-done
  555.1 0.0 slice-done.1
  555.1 7.0 constant_dynamic-update-slice_fusion.4
  562.2 8.0 constant_dynamic-update-slice_fusion.3
  570.2 8.0 constant_dynamic-update-slice_fusion.2
  578.2 7.0 constant_dynamic-update-slice_fusion.1
  585.2 6.9 constant_dynamic-update-slice_fusion
  592.1 145.4 %fusion = bf16[2,8192,1024]{2,0,1:T(2,128)(2,1)} fusion(bf16[1,2,8192,1024]{3,2,1,0:T(8,128)(2,1)} %param.5, bf16[2,16384,1024]{2,0,1:T(2,128)(2,1)} %constant_dynamic-update-slice_fusion, s32[]{:T(128)S(6)} %select_n.80, bf16[2,2]{1,0:T(2,128)(2,1)S(1)} %fusion.49), kind=kOutput, calls=%fused_computation.1 | convolution fusion | flops 150994944 | bytes 100663312 | tf_op jit(solution)/shard_map/tsb,ct->csb/dot_general | solution.py:59
  737.4 17.1 %broadcast_select_fusion.1 = (bf16[2,8192,256]{2,0,1:T(2,128)(2,1)}, bf16[2,8192,256]{2,0,1:T(2,128)(2,1)}) fusion(pred[]{:T(512)S(6)} %eq.14, bf16[2,8192,1024]{2,0,1:T(2,128)(2,1)} %fusion, s32[]{:T(128)S(6)} %select_n.85, s32[]{:T(128)S(6)} %select_n.91, pred[]{:T(512)S(6)} %eq.15), kind=kLoop, calls=%fused_computation.8 | loop fusion | flops 8388608 | bytes 33554440 | tf_op jit(solution)/shard_map/jit(_where)/select_n | solution.py:33
  754.5 0.0 all-reduce.3.cloned.1.call-update
  755.8 23.4 %copy.23 = bf16[1,2,8192,1024]{3,2,1,0:T(8,128)(2,1)} copy(bf16[1,2,8192,1024]{3,1,2,0:T(2,128)(2,1)} %bitcast.59) | data formatting | bytes 67108864
  779.2 6.3 constant_dynamic-slice_fusion.3
  785.5 478.6 %all-reduce.3.cloned.1.call-done = (bf16[2,8192,256]{2,0,1:T(2,128)(2,1)}, bf16[2,8192,256]{2,0,1:T(2,128)(2,1)}) async-done(((bf16[2,8192,256]{2,0,1:T(2,128)(2,1)}, bf16[2,8192,256]{2,0,1:T(2,128)(2,1)}), (bf16[2,8192,256]{2,0,1:T(2,128)(2,1)}, bf16[2,8192,256]{2,0,1:T(2,128)(2,1)})) %all-reduce.3.cloned.1.call-update) | async-done | bytes 16777232 | tf_op jit(solution)/shard_map/psum | solution.py:34
  1264.2 33.0 %fusion.51 = (bf16[1,8192,256]{2,0,1:T(2,128)(2,1)}, bf16[1,8192,256]{2,0,1:T(2,128)(2,1)}, bf16[1,8192,256]{2,0,1:T(2,128)(2,1)}, bf16[1,8192,256]{2,0,1:T(2,128)(2,1)}) fusion(bf16[2,8192,256]{2,0,1:T(2,128)(2,1)} %get-tuple-element.12, bf16[2,8192,256]{2,0,1:T(2,128)(2,1)} %get-tuple-element.13), kind=kLoop, calls=%fused_computation.77 | loop fusion | bytes 33554432 | tf_op jit(solution)/shard_map/slice | solution.py:43
  1297.2 0.0 copy-start.1
  1297.2 19.5 %fusion.14 = f32[1024,8192]{1,0:T(8,128)} fusion(bf16[1,8192,256]{2,0,1:T(2,128)(2,1)} %get-tuple-element.28, bf16[1,256,1024]{2,0,1:T(2,128)(2,1)} %get-tuple-element.17), kind=kOutput, calls=%fused_computation.19 | convolution fusion | flops 4294967296 | bytes 38273024 | tf_op jit(solution)/shard_map/dot_general | solution.py:41
  1316.7 0.0 copy-done.1
  1316.7 16.7 %fusion.16 = f32[1024,8192]{1,0:T(8,128)} fusion(bf16[1,8192,256]{2,0,1:T(2,128)(2,1)} %get-tuple-element.29, bf16[1,256,1024]{2,0,1:T(2,128)(2,1)S(1)} %copy-done.1), kind=kOutput, calls=%fused_computation.21 | convolution fusion | flops 4294967296 | bytes 38273024 | tf_op jit(solution)/shard_map/dot_general | solution.py:41
  1333.4 16.5 %fusion.18 = f32[1024,8192]{1,0:T(8,128)} fusion(bf16[1,8192,256]{2,0,1:T(2,128)(2,1)} %get-tuple-element.29, bf16[1,256,1024]{2,0,1:T(2,128)(2,1)S(1)} %get-tuple-element.16), kind=kOutput, calls=%fused_computation.23 | convolution fusion | flops 4294967296 | bytes 38273024 | tf_op jit(solution)/shard_map/dot_general | solution.py:41
  1349.9 16.5 %fusion.12 = f32[1024,8192]{1,0:T(8,128)} fusion(bf16[1,8192,256]{2,0,1:T(2,128)(2,1)} %get-tuple-element.28, bf16[1,256,1024]{2,0,1:T(2,128)(2,1)S(1)} %get-tuple-element.16), kind=kOutput, calls=%fused_computation.17 | convolution fusion | flops 4294967296 | bytes 38273024 | tf_op jit(solution)/shard_map/dot_general | solution.py:41
  1366.5 16.6 %fusion.10 = f32[1024,8192]{1,0:T(8,128)} fusion(bf16[1,8192,256]{2,0,1:T(2,128)(2,1)} %get-tuple-element.20, bf16[1,256,1024]{2,0,1:T(2,128)(2,1)S(1)} %get-tuple-element.15), kind=kOutput, calls=%fused_computation.15 | convolution fusion | flops 4294967296 | bytes 38273024 | tf_op jit(solution)/shard_map/dot_general | solution.py:41
  1383.0 17.7 %fusion.6 = f32[1024,8192]{1,0:T(8,128)} fusion(bf16[1,8192,256]{2,0,1:T(2,128)(2,1)} %get-tuple-element.21, bf16[1,256,1024]{2,0,1:T(2,128)(2,1)S(1)} %get-tuple-element.15), kind=kOutput, calls=%fused_computation.11 | convolution fusion | flops 4294967296 | bytes 38273024 | tf_op jit(solution)/shard_map/dot_general | solution.py:41
  1400.7 40.7 %fusion.4 = bf16[1,1,1024,8192]{3,2,1,0:T(8,128)(2,1)} fusion(f32[1024,8192]{1,0:T(8,128)} %fusion.10, f32[1024,8192]{1,0:T(8,128)} %fusion.18, f32[1024,8192]{1,0:T(8,128)} %fusion.14, bf16[1,8192,256]{2,0,1:T(2,128)(2,1)} %get-tuple-element.21, bf16[1,256,1024]{2,0,1:T(2,128)(2,1)S(1)} %get-tuple-element.14), kind=kOutput, calls=%fused_computation.9 | convolution fusion | flops 4328521728 | bytes 122159104 | tf_op jit(solution)/shard_map/dot_general | solution.py:41
  1441.4 40.7 %fusion.5 = bf16[1,1,1024,8192]{3,2,1,0:T(8,128)(2,1)} fusion(f32[1024,8192]{1,0:T(8,128)} %fusion.6, f32[1024,8192]{1,0:T(8,128)} %fusion.12, f32[1024,8192]{1,0:T(8,128)} %fusion.16, bf16[1,8192,256]{2,0,1:T(2,128)(2,1)} %get-tuple-element.20, bf16[1,256,1024]{2,0,1:T(2,128)(2,1)S(1)} %get-tuple-element.14), kind=kOutput, calls=%fused_computation.10 | convolution fusion | flops 4328521728 | bytes 122159104 | tf_op jit(solution)/shard_map/dot_general | solution.py:41
  1482.1 23.0 %pad_maximum_fusion = bf16[1,2,1024,8192]{3,2,1,0:T(8,128)(2,1)} fusion(bf16[1,1,1024,8192]{3,2,1,0:T(8,128)(2,1)} %fusion.5, bf16[1,1,1024,8192]{3,2,1,0:T(8,128)(2,1)} %fusion.4), kind=kLoop, calls=%fused_computation.3 | loop fusion | flops 16777216 | bytes 67108864 | tf_op jit(solution)/shard_map/stack | solution.py:76
  (3 shorter events, 0.0 us)
Async XLA Ops:
  7.2 1257.0 %all-reduce.3.cloned.1.call-start = ((), (), s32[]{:S(2)}) async-start(), calls=%async_computation.1 | async-start | bytes 33554432 | tf_op jit(solution)/shard_map/psum | solution.py:34
  28.2 410.5 %copy-start.2 = (s32[2]{0:T(128)S(1)}, s32[2]{0:T(128)}, u32[]{:S(2)}) copy-start(s32[2]{0:T(128)} %param.7) | copy-start | bytes 28
  28.2 416.2 %copy-start.3 = (s32[4]{0:T(128)S(1)}, s32[4]{0:T(128)}, u32[]{:S(2)}) copy-start(s32[4]{0:T(128)} %param.6) | copy-start | bytes 52
  249.3 93.1 %collective-permute-start = (bf16[2,2048,1024]{2,0,1:T(2,128)(2,1)}, bf16[2,2048,1024]{2,0,1:T(2,128)(2,1)S(1)}, u32[]{:S(2)}, u32[]{:S(2)}) collective-permute-start(bf16[2,2048,1024]{2,0,1:T(2,128)(2,1)} %bitcast.60), channel_id=1, source_target_pairs={{0,8},{8,16},{16,24},{24,0},{1,9},{9,17},{17,25},{25,1},{2,10},{10... | collective-permute-start | bytes 25165832 | tf_op jit(solution)/shard_map/ppermute | solution.py:21
  342.3 3.4 copy-start
  345.7 93.0 %collective-permute-start.1 = (bf16[2,2048,1024]{2,0,1:T(2,128)(2,1)S(1)}, bf16[2,2048,1024]{2,0,1:T(2,128)(2,1)}, u32[]{:S(2)}, u32[]{:S(2)}) collective-permute-start(bf16[2,2048,1024]{2,0,1:T(2,128)(2,1)S(1)} %collective-permute-done), channel_id=1, source_target_pairs={{0,8},{8,16},{16,24},{24,0},{1,9},{9,17},{17,25},{25,1},{2,10},{10... | collective-permute-start | bytes 25165832 | tf_op jit(solution)/shard_map/ppermute | solution.py:21
  438.7 93.2 %collective-permute-start.2 = (bf16[2,2048,1024]{2,0,1:T(2,128)(2,1)}, bf16[2,2048,1024]{2,0,1:T(2,128)(2,1)}, u32[]{:S(2)}, u32[]{:S(2)}) collective-permute-start(bf16[2,2048,1024]{2,0,1:T(2,128)(2,1)} %collective-permute-done.1), channel_id=1, source_target_pairs={{0,8},{8,16},{16,24},{24,0},{1,9},{9,17},{17,25},{25,1},{2,10},{10... | collective-permute-start | bytes 25165832 | tf_op jit(solution)/shard_map/ppermute | solution.py:21
  444.5 103.5 %slice-start.2 = ((s8[8388608]{0:T(1024)(128)(4,1)}), s8[4194304]{0:T(1024)(128)(4,1)S(1)}, s32[]{:S(2)}) async-start(s8[8388608]{0:T(1024)(128)(4,1)} %bitcast.65), calls=%async_computation.4 | async-start | bytes 8388608
  444.7 103.4 %slice-start.3 = ((s8[8388608]{0:T(1024)(128)(4,1)}), s8[4194304]{0:T(1024)(128)(4,1)S(1)}, s32[]{:S(2)}) async-start(s8[8388608]{0:T(1024)(128)(4,1)} %bitcast.65), calls=%async_computation.5 | async-start | bytes 8388608
  539.9 15.2 %slice-start = ((s8[8388608]{0:T(1024)(128)(4,1)}), s8[4194304]{0:T(1024)(128)(4,1)S(1)}, s32[]{:S(2)}) async-start(s8[8388608]{0:T(1024)(128)(4,1)} %bitcast.61), calls=%async_computation.2 | async-start | bytes 8388608
  548.1 7.1 slice-start.1
  1297.2 19.5 %copy-start.1 = (bf16[1,256,1024]{2,0,1:T(2,128)(2,1)S(1)}, bf16[1,256,1024]{2,0,1:T(2,128)(2,1)}, u32[]{:S(2)}) copy-start(bf16[1,256,1024]{2,0,1:T(2,128)(2,1)} %get-tuple-element.17) | copy-start | bytes 1572868
Sparse Core Ops, SparseCore 0:
  754.7 509.4 all-reduce.2
